TPU v7x, 32 devices: a whole 2x2x4 slice. The times are simulated.
32 devices in a mesh: rep: 4 (over x, core), frame: 4 (over z), row: 2 (over y).
Axes of the slice: x: 2, y: 2, z: 4, core: 2. Of those that a mesh axis runs over, the one named last changes fastest.
Arguments:
- activations: bfloat16 [4, 4, 16, 32, 1280], P('rep', 'frame', 'row'), may hold values from -70 to 70, as said below
- spatial_weight: bfloat16 [9, 1280, 1280], P(None, None, ('rep', 'frame')), may hold values from -0.0546875 to 0.0546875
- temporal_weight: bfloat16 [3, 1280, 1280], P(None, None, ('rep', 'frame')), may hold values from -0.09375 to 0.09375
- first_gain: float32 [1280], replicated, may hold values from 0.25 to 1.75
- first_shift: float32 [1280], replicated, may hold values from -1.5 to 1.5
- spatial_bias: float32 [1280], replicated, may hold values from -2.5 to 2.5
- second_gain: float32 [1280], replicated, may hold values from 0.25 to 1.75
- second_shift: float32 [1280], replicated, may hold values from -1.5 to 1.5
- temporal_bias: float32 [1280], replicated, may hold values from -1.5 to 1.5
Outputs:
- block_out: float32 [4, 4, 16, 32, 1280], P('rep', 'frame', 'row')
Inputs may be any that keep to these rules, and one draw needn't show every extreme that they name: `activations`: finite values.
All inputs are finite; a program needn't handle non-finite values.
Results may differ from a plain program's by a relative error of at most 0.0009.
Values may be sent and summed in bfloat16 or wider, within the bound.
No kernel may reach another device: no remote copies, remote signals or barrier semaphores. Data moves between devices by JAX's collectives and lax.ppermute only.
A program may use at most 128 MiB of HBM per device.

v0:
```python
import numpy as np
import jax
import jax.numpy as jnp
from jax import lax
from jax.sharding import PartitionSpec as P

GROUPS = 32
EPS = 1e-05


def pair_sum(value, axis):
    if lax.axis_size(axis) == 2:
        return jax.tree.map(lambda v: v + lax.ppermute(v, axis, [(0, 1), (1, 0)]), value)
    return lax.psum(value, axis)


def gather_rep(w):
    size = lax.axis_size("rep")
    if size != 4:
        return lax.all_gather(w, "rep", axis=w.ndim - 1, tiled=True)
    index = lax.axis_index("rep")
    across = lax.ppermute(w, "rep", [(k, k ^ 2) for k in range(size)])
    partner = lax.ppermute(w, "rep", [(k, k ^ 1) for k in range(size)])
    diagonal = lax.ppermute(across, "rep", [(k, k ^ 1) for k in range(size)])
    held = [w, partner, across, diagonal]
    blocks = []
    for position in range(size):
        offset = index ^ position
        block = held[3]
        for d in (2, 1, 0):
            block = jnp.where(offset == d, held[d], block)
        blocks.append(block)
    return jnp.concatenate(blocks, axis=-1)


def local_vector(vec, frame_index, rep_size, frame_size):
    width = vec.shape[0] // (rep_size * frame_size)
    table = vec.reshape(rep_size, frame_size, width)
    return lax.dynamic_index_in_dim(table, frame_index, axis=1, keepdims=False).reshape(-1)


def silu_bf16(normed):
    return jax.nn.silu(normed).astype(jnp.bfloat16)


def temporal_wide(activations, second, temporal_w, temporal_bias):
    rep_size = lax.axis_size("rep")
    frame_size = lax.axis_size("frame")
    channels = activations.shape[-1]
    _, frames, rows, cols, local = second.shape
    shard_width = local // rep_size
    second_all = lax.all_gather(second, "frame", axis=4, tiled=True)
    rows_order = np.arange(channels).reshape(rep_size, frame_size, shard_width)
    rows_order = rows_order.transpose(1, 0, 2).reshape(-1)
    temporal_w = temporal_w[:, rows_order, :]
    lhs_t = second_all.reshape(frames, rows * cols, channels)[None]
    kernel_t = temporal_w.reshape(3, 1, channels, local)
    temporal = lax.conv_general_dilated(
        lhs_t,
        kernel_t,
        window_strides=(1, 1),
        padding=((1, 1), (0, 0)),
        dimension_numbers=("NHWC", "HWIO", "NHWC"),
        preferred_element_type=jnp.float32,
    )
    temporal = temporal.reshape(1, frames, rows, cols, local).astype(jnp.bfloat16)
    back = lax.all_to_all(temporal, "frame", split_axis=1, concat_axis=4, tiled=True)
    per_frame = frames // frame_size
    back = back.reshape(1, per_frame, rows, cols, frame_size, rep_size, shard_width)
    back = jnp.swapaxes(back, 4, 5).reshape(1, per_frame, rows, cols, channels)
    return activations.astype(jnp.float32) + back.astype(jnp.float32) + temporal_bias


def shards(
    activations,
    spatial_weight,
    temporal_weight,
    first_gain,
    first_shift,
    spatial_bias,
    second_gain,
    second_shift,
    temporal_bias,
):
    rep_size = lax.axis_size("rep")
    frame_size = lax.axis_size("frame")
    row_size = lax.axis_size("row")
    frame_index = lax.axis_index("frame")
    row_index = lax.axis_index("row")
    channels = activations.shape[-1]
    rows = activations.shape[2]
    cols = activations.shape[3]
    width = channels // GROUPS
    shard_width = spatial_weight.shape[-1]
    spatial_w = gather_rep(spatial_weight)
    temporal_w = gather_rep(temporal_weight)
    local = spatial_w.shape[-1]
    raw = lax.all_gather(activations, "frame", axis=1, tiled=True)
    frames = raw.shape[1]
    if row_size > 1:
        down = [(i, i + 1) for i in range(row_size - 1)]
        up = [(i + 1, i) for i in range(row_size - 1)]
        above = lax.ppermute(raw[:, :, rows - 1 :], "row", down)
        below = lax.ppermute(raw[:, :, :1], "row", up)
    else:
        above = jnp.zeros_like(raw[:, :, :1])
        below = jnp.zeros_like(raw[:, :, :1])
    inputs = raw.astype(jnp.float32)
    grouped = inputs.reshape(1, -1, GROUPS, width)
    sums = jnp.sum(grouped, axis=(1, 3))
    squares = jnp.sum(grouped * grouped, axis=(1, 3))
    sums, squares = pair_sum((sums, squares), "row")
    count = grouped.shape[1] * width * row_size
    mean = sums / count
    variance = squares / count - mean * mean
    inverse = lax.rsqrt(variance + EPS)
    mean_full = jnp.repeat(mean, width, axis=1)[:, None, None, None, :]
    inverse_full = jnp.repeat(inverse, width, axis=1)[:, None, None, None, :]

    def first_norm(x):
        normed = (x.astype(jnp.float32) - mean_full) * inverse_full * first_gain + first_shift
        return silu_bf16(normed)

    first_mid = first_norm(raw)
    first_above = jnp.where(row_index > 0, first_norm(above), jnp.zeros((), jnp.bfloat16))
    first_below = jnp.where(
        row_index < row_size - 1, first_norm(below), jnp.zeros((), jnp.bfloat16)
    )
    padded = jnp.concatenate([first_above, first_mid, first_below], axis=2)
    field = lax.optimization_barrier(padded[0])
    spatial = None
    for col_tap in range(3):
        product = None
        for row_tap in range(3):
            term = jnp.einsum(
                "frxc,cn->frxn",
                field[:, row_tap : row_tap + rows],
                spatial_w[3 * row_tap + col_tap],
                preferred_element_type=jnp.float32,
            )
            product = term if product is None else product + term
        if col_tap == 0:
            product = jnp.pad(product[:, :, :-1], ((0, 0), (0, 0), (1, 0), (0, 0)))
        elif col_tap == 2:
            product = jnp.pad(product[:, :, 1:], ((0, 0), (0, 0), (0, 1), (0, 0)))
        spatial = product if spatial is None else spatial + product
    spatial = spatial[None]
    spatial = spatial + local_vector(spatial_bias, frame_index, rep_size, frame_size)
    g2 = local_vector(second_gain, frame_index, rep_size, frame_size)
    s2 = local_vector(second_shift, frame_index, rep_size, frame_size)
    if shard_width % width == 0:
        grouped2 = spatial.reshape(-1, local // width, width)
        sums2 = jnp.sum(grouped2, axis=(0, 2))
        squares2 = jnp.sum(grouped2 * grouped2, axis=(0, 2))
        sums2, squares2 = pair_sum((sums2, squares2), "row")
        count2 = grouped2.shape[0] * width * row_size
        mean2 = sums2 / count2
        variance2 = squares2 / count2 - mean2 * mean2
        inverse2 = lax.rsqrt(variance2 + EPS)
        mean2_full = jnp.repeat(mean2, width)
        inverse2_full = jnp.repeat(inverse2, width)
    else:
        flat = spatial.reshape(-1, local)
        csum = jnp.sum(flat, axis=0)
        csq = jnp.sum(flat * flat, axis=0)
        csum, csq = pair_sum((csum, csq), "row")
        both = lax.all_gather(jnp.stack([csum, csq]), "frame", axis=0)
        both = both.reshape(frame_size, 2, rep_size, shard_width)
        both = jnp.transpose(both, (1, 2, 0, 3)).reshape(2, GROUPS, -1)
        gsum = jnp.sum(both, axis=2)
        count2 = flat.shape[0] * row_size * width
        gmean = gsum[0] / count2
        gvar = gsum[1] / count2 - gmean * gmean
        ginv = lax.rsqrt(gvar + EPS)
        mean2_full = local_vector(jnp.repeat(gmean, width), frame_index, rep_size, frame_size)
        inverse2_full = local_vector(jnp.repeat(ginv, width), frame_index, rep_size, frame_size)
    second = silu_bf16((spatial - mean2_full) * inverse2_full * g2 + s2)
    if frame_size > 8:
        return temporal_wide(activations, second, temporal_w, temporal_bias)
    second_all = lax.all_gather(second[0], "frame", axis=0, tiled=False)
    taps = temporal_w.reshape(3, rep_size, frame_size, shard_width, local)
    temporal = None
    for group in range(frame_size):
        block = second_all[group]
        weights = taps[:, :, group].reshape(3, rep_size * shard_width, local)
        for tap in range(3):
            if tap == 1:
                source = block
            elif tap == 0:
                source = block[:-1]
            else:
                source = block[1:]
            if source.shape[0] == 0:
                continue
            term = jnp.einsum(
                "frxc,cn->frxn", source, weights[tap], preferred_element_type=jnp.float32
            )
            if tap == 0:
                term = jnp.pad(term, ((1, 0), (0, 0), (0, 0), (0, 0)))
            elif tap == 2:
                term = jnp.pad(term, ((0, 1), (0, 0), (0, 0), (0, 0)))
            temporal = term if temporal is None else temporal + term
    temporal = temporal.astype(jnp.bfloat16)
    per_frame = frames // frame_size
    result = jnp.zeros((per_frame, rows, cols, rep_size, frame_size, shard_width), jnp.float32)
    for shift in range(frame_size):
        target = (frame_index + shift) % frame_size
        piece = lax.dynamic_slice_in_dim(temporal, target * per_frame, per_frame, axis=0)
        if shift:
            piece = lax.ppermute(
                piece, "frame", [(k, (k + shift) % frame_size) for k in range(frame_size)]
            )
        source = (frame_index - shift) % frame_size
        piece = piece.reshape(per_frame, rows, cols, rep_size, 1, shard_width)
        result = lax.dynamic_update_slice_in_dim(result, piece.astype(jnp.float32), source, axis=4)
    result = result.reshape(1, per_frame, rows, cols, channels)
    return activations.astype(jnp.float32) + result + temporal_bias


def solution(mesh):
    placed = (
        P("rep", "frame", "row", None, None),
        P(None, None, ("rep", "frame")),
        P(None, None, ("rep", "frame")),
        P(),
        P(),
        P(),
        P(),
        P(),
        P(),
    )
    return jax.shard_map(
        shards,
        mesh=mesh,
        in_specs=placed,
        out_specs=P("rep", "frame", "row", None, None),
        check_vma=False,
    )
```

profile of v0, /device:TPU:0, one launch (start us, length us, event | category | flops | bytes accessed | tf_op | source)
XLA Modules:
  0.0 287.9 jit_solution(6336116725697258098)
XLA Ops:
  6.5 3.0 %collective-permute-start.5 = (bf16[9,1280,80]{1,2,0:T(8,128)(2,1)}, bf16[9,1280,80]{1,2,0:T(8,128)(2,1)S(1)}, u32[]{:S(2)}, u32[]{:S(2)}) collective-permute-start(bf16[9,1280,80]{1,2,0:T(8,128)(2,1)} %param.10), channel_id=1, source_target_pairs={{0,16},{8,24},{16,0},{24,8},{1,17},{9,25},{17,1},{25,9},{2,18},{10... | collective-permute-start | bytes 5529608 | tf_op jit(solution)/shard_map/ppermute | solution.py:22
  9.5 40.4 %collective-permute-done.5 = bf16[9,1280,80]{1,2,0:T(8,128)(2,1)S(1)} collective-permute-done((bf16[9,1280,80]{1,2,0:T(8,128)(2,1)}, bf16[9,1280,80]{1,2,0:T(8,128)(2,1)S(1)}, u32[]{:S(2)}, u32[]{:S(2)}) %collective-permute-start.5) | collective-permute-done | bytes 1843232 | tf_op jit(solution)/shard_map/ppermute | solution.py:22
  53.8 3.0 %select_select_fusion.3 = (bf16[9,1280,80]{1,2,0:T(8,128)(2,1)S(1)}, bf16[9,1280,80]{1,2,0:T(8,128)(2,1)S(1)}, bf16[9,1280,80]{1,2,0:T(8,128)(2,1)S(1)}, bf16[9,1280,80]{1,2,0:T(8,128)(2,1)S(1)}) fusion(bf16[9,1280,80]{1,2,0:T(8,128)(2,1)} %param.10, bf16[9,1280,80]{1,2,0:T(8,128)(2,1)} %collective-permute-done.4, ...), kind=kLoop, calls=%fused_computation.19 | loop fusion | flops 11059200 | bytes 14745612 | tf_op jit(solution)/shard_map/jit(_where)/select_n | solution.py:31
  56.9 6.8 %pad_maximum_fusion = bf16[9,1280,320]{1,2,0:T(8,128)(2,1)} fusion(bf16[9,1280,80]{1,2,0:T(8,128)(2,1)S(1)} %get-tuple-element.13, bf16[9,1280,80]{1,2,0:T(8,128)(2,1)S(1)} %get-tuple-element.14, bf16[9,1280,80]{1,2,0:T(8,128)(2,1)S(1)} %get-tuple-element.12, bf16[9,1280,80]{1,2,0:T(8,128)(2,1)S(1)} %get-tuple-element.11), kind=kLoop, calls=%fused_computation.3 | loop fusion | flops 29491200 | bytes 14745600 | tf_op jit(solution)/shard_map/concatenate | solution.py:33
  63.7 42.8 %all-gather.4.cloned.1.call-done = bf16[1,4,8,32,1280]{4,3,2,0,1:T(8,128)(2,1)} async-done(((bf16[1,1,8,32,1280]{4,3,2,0,1:T(8,128)(2,1)}), bf16[1,4,8,32,1280]{4,3,2,0,1:T(8,128)(2,1)}) %all-gather.4.cloned.1.call-update) | async-done | bytes 2621456 | tf_op jit(solution)/shard_map/all_gather | solution.py:98
  106.5 2.6 convert_reduce_fusion
  111.7 4.1 %collective-permute-start = (bf16[1,4,1,32,1280]{4,3,2,1,0:T(8,128)(2,1)S(1)}, bf16[1,4,1,32,1280]{4,3,2,1,0:T(8,128)(2,1)}, u32[]{:S(2)}, u32[]{:S(2)}) collective-permute-start(bf16[1,4,1,32,1280]{4,3,2,1,0:T(8,128)(2,1)S(1)} %get-tuple-element.31), channel_id=1, source_target_pairs={{0,1},{2,3},{4,5},{6,7},{8,9},{10,11},{12,13},{14,15},{16,17},{18,... | collective-permute-start | bytes 983048 | tf_op jit(solution)/shard_map/ppermute | solution.py:103
  119.5 1.9 collective-permute-done
  121.3 4.9 %collective-permute-done.3 = bf16[1,4,1,32,1280]{4,3,2,1,0:T(8,128)(2,1)} collective-permute-done((bf16[1,4,1,32,1280]{4,3,2,1,0:T(8,128)(2,1)S(1)}, bf16[1,4,1,32,1280]{4,3,2,1,0:T(8,128)(2,1)}, u32[]{:S(2)}, u32[]{:S(2)}) %collective-permute-start.3) | collective-permute-done | bytes 327712 | tf_op jit(solution)/shard_map/ppermute | solution.py:104
  128.4 2.9 fusion.13
  143.1 2.2 multiply_reduce_fusion
  145.8 2.1 collective-permute-start.8
  152.7 11.2 %collective-permute-done.10 = bf16[3,1280,80]{1,2,0:T(8,128)(2,1)} collective-permute-done((bf16[3,1280,80]{1,2,0:T(8,128)(2,1)S(1)}, bf16[3,1280,80]{1,2,0:T(8,128)(2,1)}, u32[]{:S(2)}, u32[]{:S(2)}) %collective-permute-start.10) | collective-permute-done | bytes 614432 | tf_op jit(solution)/shard_map/ppermute | solution.py:22
  167.8 2.2 copy.65
  171.6 2.8 pad_maximum_fusion.1
  174.8 39.5 %all-gather.6.cloned.1.call-done = bf16[16,8,32,320]{3,2,1,0:T(8,128)(2,1)} async-done(((bf16[4,8,32,320]{3,2,1,0:T(8,128)(2,1)}), bf16[16,8,32,320]{3,2,1,0:T(8,128)(2,1)}) %all-gather.6.cloned.1.call-update) | async-done | bytes 2621456 | tf_op jit(solution)/shard_map/all_gather | solution.py:180
  214.3 1.8 fusion.25
  226.3 2.7 collective-permute-start.14
  229.7 11.4 %dynamic_update_slice.12 = f32[1,8,32,4,4,80]{5,4,3,2,1,0:T(4,128)S(1)} dynamic-update-slice(f32[1,8,32,4,4,80]{5,4,3,2,1,0:T(4,128)S(1)} %broadcast_in_dim.32, f32[1,8,32,4,1,80]{5,4,3,2,1,0:T(1,128)S(1)} %bitcast.222, s32[]{:T(128)} %constant.81.clone.1, s32[]{:T(128)} %constant.81.clone.1, s32[]{:T(128)} %constant.81.clone.1, s32[]{:T(128)} %constant.81.clone.1, s32[]{:T(128)S(6)} %select_n.277, ...) | dynamic-update-slice | bytes 655364 | tf_op jit(solution)/shard_map/dynamic_update_slice | solution.py:215
  241.5 11.4 %dynamic_update_slice.13 = f32[1,8,32,4,4,80]{5,4,3,2,1,0:T(4,128)S(1)} dynamic-update-slice(f32[1,8,32,4,4,80]{5,4,3,2,1,0:T(4,128)S(1)} %dynamic_update_slice.12, f32[1,8,32,4,1,80]{5,4,3,2,1,0:T(1,128)S(1)} %bitcast.224, s32[]{:T(128)} %constant.81.clone.1, s32[]{:T(128)} %constant.81.clone.1, s32[]{:T(128)} %constant.81.clone.1, s32[]{:T(128)} %constant.81.clone.1, s32[]{:T(128)S(6)} %select_n.281, ...) | dynamic-update-slice | bytes 655364 | tf_op jit(solution)/shard_map/dynamic_update_slice | solution.py:215
  253.3 11.4 %dynamic_update_slice.14 = f32[1,8,32,4,4,80]{5,4,3,2,1,0:T(4,128)S(1)} dynamic-update-slice(f32[1,8,32,4,4,80]{5,4,3,2,1,0:T(4,128)S(1)} %dynamic_update_slice.13, f32[1,8,32,4,1,80]{5,4,3,2,1,0:T(1,128)S(1)} %bitcast.225, s32[]{:T(128)} %constant.81.clone.1, s32[]{:T(128)} %constant.81.clone.1, s32[]{:T(128)} %constant.81.clone.1, s32[]{:T(128)} %constant.81.clone.1, s32[]{:T(128)S(6)} %select_n.285, ...) | dynamic-update-slice | bytes 655364 | tf_op jit(solution)/shard_map/dynamic_update_slice | solution.py:215
  265.1 11.4 %dynamic_update_slice.15 = f32[1,8,32,4,4,80]{5,4,3,2,1,0:T(4,128)S(1)} dynamic-update-slice(f32[1,8,32,4,4,80]{5,4,3,2,1,0:T(4,128)S(1)} %dynamic_update_slice.14, f32[1,8,32,4,1,80]{5,4,3,2,1,0:T(1,128)S(1)} %bitcast.223, s32[]{:T(128)} %constant.81.clone.1, s32[]{:T(128)} %constant.81.clone.1, s32[]{:T(128)} %constant.81.clone.1, s32[]{:T(128)} %constant.81.clone.1, s32[]{:T(128)S(6)} %select_n.289, ...) | dynamic-update-slice | bytes 655364 | tf_op jit(solution)/shard_map/dynamic_update_slice | solution.py:215
  276.5 2.2 reshape.184
  278.8 2.3 add_add_fusion.1
  (104 shorter events, 46.8 us)
Async XLA Ops:
  6.5 99.9 %all-gather.4.cloned.1.call-start = ((), (), s32[]{:S(2)}) async-start(), calls=%async_computation | async-start | bytes 3276800 | tf_op jit(solution)/shard_map/all_gather | solution.py:98
  6.5 43.4 %collective-permute-start.5 = (bf16[9,1280,80]{1,2,0:T(8,128)(2,1)}, bf16[9,1280,80]{1,2,0:T(8,128)(2,1)S(1)}, u32[]{:S(2)}, u32[]{:S(2)}) collective-permute-start(bf16[9,1280,80]{1,2,0:T(8,128)(2,1)} %param.10), channel_id=1, source_target_pairs={{0,16},{8,24},{16,0},{24,8},{1,17},{9,25},{17,1},{25,9},{2,18},{10... | collective-permute-start | bytes 5529608 | tf_op jit(solution)/shard_map/ppermute | solution.py:22
  9.5 43.2 %collective-permute-start.4 = (bf16[9,1280,80]{1,2,0:T(8,128)(2,1)}, bf16[9,1280,80]{1,2,0:T(8,128)(2,1)}, u32[]{:S(2)}, u32[]{:S(2)}) collective-permute-start(bf16[9,1280,80]{1,2,0:T(8,128)(2,1)} %param.10), channel_id=1, source_target_pairs={{0,8},{8,0},{16,24},{24,16},{1,9},{9,1},{17,25},{25,17},{2,10},{10... | collective-permute-start | bytes 5529608 | tf_op jit(solution)/shard_map/ppermute | solution.py:23
  49.9 3.9 %collective-permute-start.6 = (bf16[9,1280,80]{1,2,0:T(8,128)(2,1)S(1)}, bf16[9,1280,80]{1,2,0:T(8,128)(2,1)}, u32[]{:S(2)}, u32[]{:S(2)}) collective-permute-start(bf16[9,1280,80]{1,2,0:T(8,128)(2,1)S(1)} %collective-permute-done.5), channel_id=1, source_target_pairs={{0,8},{8,0},{16,24},{24,16},{1,9},{9,1},{17,25},{25,17},{2,10},{10... | collective-permute-start | bytes 5529608 | tf_op jit(solution)/shard_map/ppermute | solution.py:24
  49.9 164.4 %all-gather.6.cloned.1.call-start = ((), (), s32[]{:S(2)}) async-start(), calls=%async_computation.1 | async-start | bytes 3932160 | tf_op jit(solution)/shard_map/all_gather | solution.py:180
  63.6 54.0 %copy-start.3 = (f32[1280]{0:T(1024)S(1)}, f32[1280]{0:T(1024)}, u32[]{:S(2)}) copy-start(f32[1280]{0:T(1024)} %param.13) | copy-start | bytes 15364
  63.6 54.0 %copy-start.4 = (f32[1280]{0:T(1024)S(1)}, f32[1280]{0:T(1024)}, u32[]{:S(2)}) copy-start(f32[1280]{0:T(1024)} %param.12) | copy-start | bytes 15364
  106.5 5.2 %copy-start.1 = (bf16[1,4,8,32,1280]{4,3,2,0,1:T(8,128)(2,1)S(1)}, bf16[1,4,8,32,1280]{4,3,2,0,1:T(8,128)(2,1)}, u32[]{:S(2)}) copy-start(bf16[1,4,8,32,1280]{4,3,2,0,1:T(8,128)(2,1)} %all-gather.4.cloned.1.call-done) | copy-start | bytes 7864324
  109.3 8.0 %collective-permute-start.1 = (f32[1,32]{1,0:T(1,128)S(1)}, f32[1,32]{1,0:T(1,128)S(1)}, u32[]{:S(2)}, u32[]{:S(2)}) collective-permute-start(f32[1,32]{1,0:T(1,128)S(1)} %bitcast.238), channel_id=1, source_target_pairs={{0,1},{1,0},{2,3},{3,2},{4,5},{5,4},{6,7},{7,6},{8,9},{9,8},{10,11... | collective-permute-start | bytes 392 | tf_op jit(solution)/shard_map/ppermute | solution.py:13
  111.1 6.2 %collective-permute-start.2 = (f32[1,32]{1,0:T(1,128)S(1)}, f32[1,32]{1,0:T(1,128)S(1)}, u32[]{:S(2)}, u32[]{:S(2)}) collective-permute-start(f32[1,32]{1,0:T(1,128)S(1)} %bitcast.239), channel_id=1, source_target_pairs={{0,1},{1,0},{2,3},{3,2},{4,5},{5,4},{6,7},{7,6},{8,9},{9,8},{10,11... | collective-permute-start | bytes 392 | tf_op jit(solution)/shard_map/ppermute | solution.py:13
  111.7 9.6 %collective-permute-start = (bf16[1,4,1,32,1280]{4,3,2,1,0:T(8,128)(2,1)S(1)}, bf16[1,4,1,32,1280]{4,3,2,1,0:T(8,128)(2,1)}, u32[]{:S(2)}, u32[]{:S(2)}) collective-permute-start(bf16[1,4,1,32,1280]{4,3,2,1,0:T(8,128)(2,1)S(1)} %get-tuple-element.31), channel_id=1, source_target_pairs={{0,1},{2,3},{4,5},{6,7},{8,9},{10,11},{12,13},{14,15},{16,17},{18,... | collective-permute-start | bytes 983048 | tf_op jit(solution)/shard_map/ppermute | solution.py:103
  115.8 10.4 %collective-permute-start.3 = (bf16[1,4,1,32,1280]{4,3,2,1,0:T(8,128)(2,1)S(1)}, bf16[1,4,1,32,1280]{4,3,2,1,0:T(8,128)(2,1)}, u32[]{:S(2)}, u32[]{:S(2)}) collective-permute-start(bf16[1,4,1,32,1280]{4,3,2,1,0:T(8,128)(2,1)S(1)} %get-tuple-element.32), channel_id=1, source_target_pairs={{1,0},{3,2},{5,4},{7,6},{9,8},{11,10},{13,12},{15,14},{17,16},{19,... | collective-permute-start | bytes 983048 | tf_op jit(solution)/shard_map/ppermute | solution.py:104
  126.3 5.0 %slice-start = ((s8[7372800]{0:T(1024)(128)(4,1)}), s8[4194304]{0:T(1024)(128)(4,1)S(1)}, s32[]{:S(2)}) async-start(s8[7372800]{0:T(1024)(128)(4,1)} %bitcast.219), calls=%async_computation.2 | async-start | bytes 8388608
  128.0 3.3 %slice-start.1 = ((s8[7372800]{0:T(1024)(128)(4,1)}), s8[3178496]{0:T(1024)(128)(4,1)S(1)}, s32[]{:S(2)}) async-start(s8[7372800]{0:T(1024)(128)(4,1)} %bitcast.219), calls=%async_computation.3 | async-start | bytes 6356992
  145.3 5.9 %copy-start.2 = (bf16[3,1280,80]{1,2,0:T(8,128)(2,1)S(1)}, bf16[3,1280,80]{1,2,0:T(8,128)(2,1)}, u32[]{:S(2)}) copy-start(bf16[3,1280,80]{1,2,0:T(8,128)(2,1)} %param.11) | copy-start | bytes 1843204
  145.5 3.6 %collective-permute-start.7 = (f32[8]{0:T(128)S(1)}, f32[8]{0:T(128)S(1)}, u32[]{:S(2)}, u32[]{:S(2)}) collective-permute-start(f32[8]{0:T(128)S(1)} %reduce_sum.78), channel_id=1, source_target_pairs={{0,1},{1,0},{2,3},{3,2},{4,5},{5,4},{6,7},{7,6},{8,9},{9,8},{10,11... | collective-permute-start | bytes 104 | tf_op jit(solution)/shard_map/ppermute | solution.py:13
  145.8 3.6 %collective-permute-start.8 = (f32[8]{0:T(128)S(1)}, f32[8]{0:T(128)S(1)}, u32[]{:S(2)}, u32[]{:S(2)}) collective-permute-start(f32[8]{0:T(128)S(1)} %reduce_sum.81), channel_id=1, source_target_pairs={{0,1},{1,0},{2,3},{3,2},{4,5},{5,4},{6,7},{7,6},{8,9},{9,8},{10,11... | collective-permute-start | bytes 104 | tf_op jit(solution)/shard_map/ppermute | solution.py:13
  151.2 12.7 %collective-permute-start.10 = (bf16[3,1280,80]{1,2,0:T(8,128)(2,1)S(1)}, bf16[3,1280,80]{1,2,0:T(8,128)(2,1)}, u32[]{:S(2)}, u32[]{:S(2)}) collective-permute-start(bf16[3,1280,80]{1,2,0:T(8,128)(2,1)S(1)} %copy-done.2), channel_id=1, source_target_pairs={{0,16},{8,24},{16,0},{24,8},{1,17},{9,25},{17,1},{25,9},{2,18},{10... | collective-permute-start | bytes 1843208 | tf_op jit(solution)/shard_map/ppermute | solution.py:22
  152.7 13.5 %collective-permute-start.9 = (bf16[3,1280,80]{1,2,0:T(8,128)(2,1)S(1)}, bf16[3,1280,80]{1,2,0:T(8,128)(2,1)}, u32[]{:S(2)}, u32[]{:S(2)}) collective-permute-start(bf16[3,1280,80]{1,2,0:T(8,128)(2,1)S(1)} %copy-done.2), channel_id=1, source_target_pairs={{0,8},{8,0},{16,24},{24,16},{1,9},{9,1},{17,25},{25,17},{2,10},{10... | collective-permute-start | bytes 1843208 | tf_op jit(solution)/shard_map/ppermute | solution.py:23
  163.9 3.8 %collective-permute-start.11 = (bf16[3,1280,80]{1,2,0:T(8,128)(2,1)}, bf16[3,1280,80]{1,2,0:T(8,128)(2,1)}, u32[]{:S(2)}, u32[]{:S(2)}) collective-permute-start(bf16[3,1280,80]{1,2,0:T(8,128)(2,1)} %collective-permute-done.10), channel_id=1, source_target_pairs={{0,8},{8,0},{16,24},{24,16},{1,9},{9,1},{17,25},{25,17},{2,10},{10... | collective-permute-start | bytes 1843208 | tf_op jit(solution)/shard_map/ppermute | solution.py:24
  214.3 3.4 %copy-start = (bf16[16,8,32,320]{3,2,1,0:T(8,128)(2,1)S(1)}, bf16[16,8,32,320]{3,2,1,0:T(8,128)(2,1)}, u32[]{:S(2)}) copy-start(bf16[16,8,32,320]{3,2,1,0:T(8,128)(2,1)} %all-gather.6.cloned.1.call-done) | copy-start | bytes 7864324
  225.0 16.1 %collective-permute-start.12 = (bf16[1,8,32,320]{3,2,1,0:T(8,128)(2,1)}, bf16[1,8,32,320]{3,2,1,0:T(8,128)(2,1)S(1)}, u32[]{:S(2)}, u32[]{:S(2)}) collective-permute-start(bf16[1,8,32,320]{3,2,1,0:T(8,128)(2,1)} %get-tuple-element.35), channel_id=1, source_target_pairs={{0,2},{2,4},{4,6},{6,0},{1,3},{3,5},{5,7},{7,1},{8,10},{10,12},{12... | collective-permute-start | bytes 491528 | tf_op jit(solution)/shard_map/ppermute | solution.py:210
  225.0 27.9 %collective-permute-start.13 = (bf16[1,8,32,320]{3,2,1,0:T(8,128)(2,1)}, bf16[1,8,32,320]{3,2,1,0:T(8,128)(2,1)S(1)}, u32[]{:S(2)}, u32[]{:S(2)}) collective-permute-start(bf16[1,8,32,320]{3,2,1,0:T(8,128)(2,1)} %get-tuple-element.34), channel_id=1, source_target_pairs={{0,4},{2,6},{4,0},{6,2},{1,5},{3,7},{5,1},{7,3},{8,12},{10,14},{12... | collective-permute-start | bytes 491528 | tf_op jit(solution)/shard_map/ppermute | solution.py:210
  226.3 38.4 %collective-permute-start.14 = (bf16[1,8,32,320]{3,2,1,0:T(8,128)(2,1)S(1)}, bf16[1,8,32,320]{3,2,1,0:T(8,128)(2,1)S(1)}, u32[]{:S(2)}, u32[]{:S(2)}) collective-permute-start(bf16[1,8,32,320]{3,2,1,0:T(8,128)(2,1)S(1)} %get-tuple-element.33), channel_id=1, source_target_pairs={{0,6},{2,0},{4,2},{6,4},{1,7},{3,1},{5,3},{7,5},{8,14},{10,8},{12,... | collective-permute-start | bytes 491528 | tf_op jit(solution)/shard_map/ppermute | solution.py:210
  (1 other events, 2.3 us)
Sparse Core Ops, SparseCore 0:
  50.0 56.3 all-gather.3
  151.3 62.9 all-gather.5
where the time goes:
time: 288 us
  waiting for transfers between devices  143 us (50%)
  local copies, waits for them, and re-layouts  59.6 us (21%)
  other arithmetic  27 us (9%)
  matrix products  25.5 us (9%)
  starting transfers between devices  18.4 us (6%)
  between operations  14 us (5%)
    ppermute x2, waiting for transfers between devices, gather_rep(): across = lax.ppermute(w, 'rep', [(k, k ^ 2) for k in range(size)])  51.6 us
    dynamic_update_slice x4, local copies, waits for them, and re-layouts, shards(): lax.dynamic_update_slice_in_dim(result, piece.astype(jnp.float32), source...  45.8 us
    all_gather x1, waiting for transfers between devices, shards(): raw = lax.all_gather(activations, 'frame', axis=1, tiled=True)  42.8 us
    all_gather x1, waiting for transfers between devices, shards(): second_all = lax.all_gather(second[0], 'frame', axis=0, tiled=False)  39.5 us
    dot_general x9, matrix products, shards(): jnp.einsum('frxc,cn->frxn', field[:, row_tap:row_tap + rows], spatial_w[3...  15.8 us
    concatenate x2, other arithmetic, gather_rep(): return jnp.concatenate(blocks, axis=-1)  9.57 us
    dot_general x8, matrix products, shards(): jnp.einsum('frxc,cn->frxn', source, weights[tap], preferred_element_type=...  6.05 us
  transfers between devices with their start and end apart: 17, of which 9 were waited for; matrix products, arithmetic and copies ran while one was open for 21% of the time, Pallas kernels for 0%

commit v1 on v0

--- a/solution.py
+++ b/solution.py
@@ -95,7 +95,14 @@
     spatial_w = gather_rep(spatial_weight)
     temporal_w = gather_rep(temporal_weight)
     local = spatial_w.shape[-1]
-    raw = lax.all_gather(activations, "frame", axis=1, tiled=True)
+    x_2 = activations
+    ways, here, hop = (lax.axis_size("frame"), lax.axis_index("frame"), x_2.shape[1])
+    lengths = [n * ways if d_2 == 1 else n for d_2, n in enumerate(x_2.shape)]
+    full = lax.dynamic_update_slice_in_dim(jnp.zeros(lengths, x_2.dtype), x_2, here * hop, axis=1)
+    for far in range(1, ways):
+        x_2 = lax.ppermute(x_2, "frame", [(d_2, (d_2 + 1) % ways) for d_2 in range(ways)])
+        full = lax.dynamic_update_slice_in_dim(full, x_2, (here - far) % ways * hop, axis=1)
+    raw = full
     frames = raw.shape[1]
     if row_size > 1:
         down = [(i, i + 1) for i in range(row_size - 1)]

time: 288 us -> 248 us (0.86)
  waiting for transfers between devices: 143 us -> 102 us
  local copies, waits for them, and re-layouts: 59.6 us -> 63.3 us
  other arithmetic: 27 us -> 24 us
    all_gather x1 -> x0, waiting for transfers between devices: 42.8 us -> none  [shards(): raw = lax.all_gather(activations, 'frame', axis=1, tiled=True)]
    ppermute x0 -> x3, waiting for transfers between devices: none -> 40.5 us  [shards(): lax.ppermute(x_2, 'frame', [(d_2, (d_2 + 1) % ways) for d_2 in range(ways)])]
    ppermute x2, waiting for transfers between devices: 51.6 us -> 13.6 us  [gather_rep(): across = lax.ppermute(w, 'rep', [(k, k ^ 2) for k in range(size)])]
    ppermute x0 -> x3, starting transfers between devices: none -> 3.06 us  [shards(): lax.ppermute(x_2, 'frame', [(d_2, (d_2 + 1) % ways) for d_2 in range(ways)])]
  transfers between devices with their start and end apart: 17 -> 19, of which waited for: 9 -> 10; matrix products, arithmetic and copies ran while one was open for 21% -> 23% of each run, Pallas kernels for 0% -> 0%
where the time goes in v1:
time: 248 us; the launch traced here: 247 us
  waiting for transfers between devices  102 us (41%)
  local copies, waits for them, and re-layouts  63.3 us (26%)
  other arithmetic  24 us (10%)
  matrix products  23.9 us (10%)
  starting transfers between devices  19.5 us (8%)
  between operations  14.1 us (6%)
    dynamic_update_slice x4, local copies, waits for them, and re-layouts, shards(): lax.dynamic_update_slice_in_dim(result, piece.astype(jnp.float32), source...  46 us
    all_gather x1, waiting for transfers between devices, shards(): second_all = lax.all_gather(second[0], 'frame', axis=0, tiled=False)  40.9 us
    ppermute x3, waiting for transfers between devices, shards(): lax.ppermute(x_2, 'frame', [(d_2, (d_2 + 1) % ways) for d_2 in range(ways)])  40.5 us
    dot_general x9, matrix products, shards(): jnp.einsum('frxc,cn->frxn', field[:, row_tap:row_tap + rows], spatial_w[3...  14.2 us
    ppermute x2, waiting for transfers between devices, gather_rep(): across = lax.ppermute(w, 'rep', [(k, k ^ 2) for k in range(size)])  13.6 us
    concatenate x2, other arithmetic, gather_rep(): return jnp.concatenate(blocks, axis=-1)  8.68 us
    dot_general x8, matrix products, shards(): jnp.einsum('frxc,cn->frxn', source, weights[tap], preferred_element_type=...  6.05 us
    ppermute x1, waiting for transfers between devices, shards(): below = lax.ppermute(raw[:, :, :1], 'row', up)  5.24 us
  transfers between devices with their start and end apart: 19, of which 10 were waited for; matrix products, arithmetic and copies ran while one was open for 23% of the time, Pallas kernels for 0%

profile of v1, /device:TPU:0, one launch (start us, length us, event | category | flops | bytes accessed | tf_op | source)
XLA Modules:
  0.0 247.0 jit_solution(17293686733206280084)
XLA Ops:
  6.5 3.1 %collective-permute-start = (bf16[1,1,8,32,1280]{4,3,2,1,0:T(8,128)(2,1)}, bf16[1,1,8,32,1280]{4,3,2,1,0:T(8,128)(2,1)S(1)}, u32[]{:S(2)}, u32[]{:S(2)}) collective-permute-start(bf16[1,1,8,32,1280]{4,3,2,1,0:T(8,128)(2,1)} %param.9), channel_id=1, source_target_pairs={{0,2},{2,4},{4,6},{6,0},{1,3},{3,5},{5,7},{7,1},{8,10},{10,12},{12... | collective-permute-start | bytes 1966088 | tf_op jit(solution)/shard_map/ppermute | solution.py:103
  11.1 15.5 %collective-permute-done = bf16[1,1,8,32,1280]{4,3,2,1,0:T(8,128)(2,1)S(1)} collective-permute-done((bf16[1,1,8,32,1280]{4,3,2,1,0:T(8,128)(2,1)}, bf16[1,1,8,32,1280]{4,3,2,1,0:T(8,128)(2,1)S(1)}, u32[]{:S(2)}, u32[]{:S(2)}) %collective-permute-start) | collective-permute-done | bytes 655392 | tf_op jit(solution)/shard_map/ppermute | solution.py:103
  29.4 15.0 %collective-permute-done.1 = bf16[1,1,8,32,1280]{4,3,2,1,0:T(8,128)(2,1)} collective-permute-done((bf16[1,1,8,32,1280]{4,3,2,1,0:T(8,128)(2,1)S(1)}, bf16[1,1,8,32,1280]{4,3,2,1,0:T(8,128)(2,1)}, u32[]{:S(2)}, u32[]{:S(2)}) %collective-permute-start.1) | collective-permute-done | bytes 655392 | tf_op jit(solution)/shard_map/ppermute | solution.py:103
  46.7 4.8 %collective-permute-done.8 = bf16[9,1280,80]{1,2,0:T(8,128)(2,1)} collective-permute-done((bf16[9,1280,80]{1,2,0:T(8,128)(2,1)}, bf16[9,1280,80]{1,2,0:T(8,128)(2,1)}, u32[]{:S(2)}, u32[]{:S(2)}) %collective-permute-start.8) | collective-permute-done | bytes 1843232 | tf_op jit(solution)/shard_map/ppermute | solution.py:22
  51.6 9.9 %collective-permute-done.2 = bf16[1,1,8,32,1280]{4,3,2,1,0:T(8,128)(2,1)S(1)} collective-permute-done((bf16[1,1,8,32,1280]{4,3,2,1,0:T(8,128)(2,1)}, bf16[1,1,8,32,1280]{4,3,2,1,0:T(8,128)(2,1)S(1)}, u32[]{:S(2)}, u32[]{:S(2)}) %collective-permute-start.2) | collective-permute-done | bytes 655392 | tf_op jit(solution)/shard_map/ppermute | solution.py:103
  64.9 3.9 %collective-permute-start.3 = (bf16[1,4,1,32,1280]{4,3,2,1,0:T(8,128)(2,1)S(1)}, bf16[1,4,1,32,1280]{4,3,2,1,0:T(8,128)(2,1)}, u32[]{:S(2)}, u32[]{:S(2)}) collective-permute-start(bf16[1,4,1,32,1280]{4,3,2,1,0:T(8,128)(2,1)S(1)} %get-tuple-element.31), channel_id=1, source_target_pairs={{0,1},{2,3},{4,5},{6,7},{8,9},{10,11},{12,13},{14,15},{16,17},{18,... | collective-permute-start | bytes 983048 | tf_op jit(solution)/shard_map/ppermute | solution.py:110
  70.4 1.8 fusion.9
  72.6 5.2 %collective-permute-done.6 = bf16[1,4,1,32,1280]{4,3,2,1,0:T(8,128)(2,1)} collective-permute-done((bf16[1,4,1,32,1280]{4,3,2,1,0:T(8,128)(2,1)S(1)}, bf16[1,4,1,32,1280]{4,3,2,1,0:T(8,128)(2,1)}, u32[]{:S(2)}, u32[]{:S(2)}) %collective-permute-start.6) | collective-permute-done | bytes 327712 | tf_op jit(solution)/shard_map/ppermute | solution.py:111
  80.9 3.0 %select_select_fusion.3 = (bf16[9,1280,80]{1,2,0:T(8,128)(2,1)S(1)}, bf16[9,1280,80]{1,2,0:T(8,128)(2,1)S(1)}, bf16[9,1280,80]{1,2,0:T(8,128)(2,1)S(1)}, bf16[9,1280,80]{1,2,0:T(8,128)(2,1)S(1)}) fusion(bf16[9,1280,80]{1,2,0:T(8,128)(2,1)S(1)} %copy-done.2, bf16[9,1280,80]{1,2,0:T(8,128)(2,1)} %collective-permute-done.7, ...), kind=kLoop, calls=%fused_computation.19 | loop fusion | flops 11059200 | bytes 14745612 | tf_op jit(solution)/shard_map/jit(_where)/select_n | solution.py:31
  84.0 5.7 %pad_maximum_fusion = bf16[9,1280,320]{1,2,0:T(8,128)(2,1)S(1)} fusion(bf16[9,1280,80]{1,2,0:T(8,128)(2,1)S(1)} %get-tuple-element.13, bf16[9,1280,80]{1,2,0:T(8,128)(2,1)S(1)} %get-tuple-element.14, bf16[9,1280,80]{1,2,0:T(8,128)(2,1)S(1)} %get-tuple-element.12, bf16[9,1280,80]{1,2,0:T(8,128)(2,1)S(1)} %get-tuple-element.11), kind=kLoop, calls=%fused_computation.3 | loop fusion | flops 29491200 | bytes 14745600 | tf_op jit(solution)/shard_map/concatenate | solution.py:33
  103.0 2.0 multiply_reduce_fusion
  105.5 2.1 collective-permute-start.11
  112.4 8.8 %collective-permute-done.13 = bf16[3,1280,80]{1,2,0:T(8,128)(2,1)} collective-permute-done((bf16[3,1280,80]{1,2,0:T(8,128)(2,1)S(1)}, bf16[3,1280,80]{1,2,0:T(8,128)(2,1)}, u32[]{:S(2)}, u32[]{:S(2)}) %collective-permute-start.13) | collective-permute-done | bytes 614432 | tf_op jit(solution)/shard_map/ppermute | solution.py:22
  125.0 2.2 copy.57
  128.9 3.0 %pad_maximum_fusion.1 = bf16[3,1280,320]{2,1,0:T(8,128)(2,1)S(1)} fusion(bf16[3,1280,80]{2,1,0:T(8,128)(2,1)S(1)} %get-tuple-element.16, bf16[3,1280,80]{2,1,0:T(8,128)(2,1)S(1)} %get-tuple-element.17, bf16[3,1280,80]{2,1,0:T(8,128)(2,1)S(1)} %get-tuple-element.18, bf16[3,1280,80]{2,1,0:T(8,128)(2,1)S(1)} %get-tuple-element.15), kind=kLoop, calls=%fused_computation.15 | loop fusion | flops 9830400 | bytes 4915200 | tf_op jit(solution)/shard_map/concatenate | solution.py:33
  132.3 40.9 %all-gather.3.cloned.1.call-done = bf16[16,8,32,320]{3,2,1,0:T(8,128)(2,1)} async-done(((bf16[4,8,32,320]{3,2,1,0:T(8,128)(2,1)}), bf16[16,8,32,320]{3,2,1,0:T(8,128)(2,1)}) %all-gather.3.cloned.1.call-update) | async-done | bytes 2621456 | tf_op jit(solution)/shard_map/all_gather | solution.py:187
  173.2 1.8 fusion.25
  185.2 2.7 %collective-permute-start.17 = (bf16[1,8,32,320]{3,2,1,0:T(8,128)(2,1)S(1)}, bf16[1,8,32,320]{3,2,1,0:T(8,128)(2,1)S(1)}, u32[]{:S(2)}, u32[]{:S(2)}) collective-permute-start(bf16[1,8,32,320]{3,2,1,0:T(8,128)(2,1)S(1)} %get-tuple-element.33), channel_id=1, source_target_pairs={{0,6},{2,0},{4,2},{6,4},{1,7},{3,1},{5,3},{7,5},{8,14},{10,8},{12,... | collective-permute-start | bytes 491528 | tf_op jit(solution)/shard_map/ppermute | solution.py:217
  188.5 11.7 %dynamic_update_slice.28 = f32[1,8,32,4,4,80]{5,4,3,2,1,0:T(4,128)S(1)} dynamic-update-slice(f32[1,8,32,4,4,80]{5,4,3,2,1,0:T(4,128)S(1)} %broadcast_in_dim.35, f32[1,8,32,4,1,80]{5,4,3,2,1,0:T(1,128)S(1)} %bitcast.211, s32[]{:T(128)} %constant.88.clone.1, s32[]{:T(128)} %constant.88.clone.1, s32[]{:T(128)} %constant.88.clone.1, s32[]{:T(128)} %constant.88.clone.1, s32[]{:T(128)S(6)} %select_n.293, ...) | dynamic-update-slice | bytes 655364 | tf_op jit(solution)/shard_map/dynamic_update_slice | solution.py:222
  200.6 11.4 %dynamic_update_slice.29 = f32[1,8,32,4,4,80]{5,4,3,2,1,0:T(4,128)S(1)} dynamic-update-slice(f32[1,8,32,4,4,80]{5,4,3,2,1,0:T(4,128)S(1)} %dynamic_update_slice.28, f32[1,8,32,4,1,80]{5,4,3,2,1,0:T(1,128)S(1)} %bitcast.213, s32[]{:T(128)} %constant.88.clone.1, s32[]{:T(128)} %constant.88.clone.1, s32[]{:T(128)} %constant.88.clone.1, s32[]{:T(128)} %constant.88.clone.1, s32[]{:T(128)S(6)} %select_n.236, ...) | dynamic-update-slice | bytes 655364 | tf_op jit(solution)/shard_map/dynamic_update_slice | solution.py:222
  212.4 11.4 %dynamic_update_slice.30 = f32[1,8,32,4,4,80]{5,4,3,2,1,0:T(4,128)S(1)} dynamic-update-slice(f32[1,8,32,4,4,80]{5,4,3,2,1,0:T(4,128)S(1)} %dynamic_update_slice.29, f32[1,8,32,4,1,80]{5,4,3,2,1,0:T(1,128)S(1)} %bitcast.214, s32[]{:T(128)} %constant.88.clone.1, s32[]{:T(128)} %constant.88.clone.1, s32[]{:T(128)} %constant.88.clone.1, s32[]{:T(128)} %constant.88.clone.1, s32[]{:T(128)S(6)} %select_n.238, ...) | dynamic-update-slice | bytes 655364 | tf_op jit(solution)/shard_map/dynamic_update_slice | solution.py:222
  224.2 11.4 %dynamic_update_slice.31 = f32[1,8,32,4,4,80]{5,4,3,2,1,0:T(4,128)S(1)} dynamic-update-slice(f32[1,8,32,4,4,80]{5,4,3,2,1,0:T(4,128)S(1)} %dynamic_update_slice.30, f32[1,8,32,4,1,80]{5,4,3,2,1,0:T(1,128)S(1)} %bitcast.212, s32[]{:T(128)} %constant.88.clone.1, s32[]{:T(128)} %constant.88.clone.1, s32[]{:T(128)} %constant.88.clone.1, s32[]{:T(128)} %constant.88.clone.1, s32[]{:T(128)S(6)} %select_n.240, ...) | dynamic-update-slice | bytes 655364 | tf_op jit(solution)/shard_map/dynamic_update_slice | solution.py:222
  235.6 2.2 reshape.184
  237.9 2.3 add_add_fusion.1
  (113 shorter events, 51.1 us)
Async XLA Ops:
  6.5 38.2 %copy-start.1 = (bf16[1,1,8,32,1280]{4,3,2,1,0:T(8,128)(2,1)S(1)}, bf16[1,1,8,32,1280]{4,3,2,1,0:T(8,128)(2,1)}, u32[]{:S(2)}) copy-start(bf16[1,1,8,32,1280]{4,3,2,1,0:T(8,128)(2,1)} %param.9) | copy-start | bytes 1966084
  6.5 166.6 %all-gather.3.cloned.1.call-start = ((), (), s32[]{:S(2)}) async-start(), calls=%async_computation | async-start | bytes 3932160 | tf_op jit(solution)/shard_map/all_gather | solution.py:187
  6.5 20.1 %collective-permute-start = (bf16[1,1,8,32,1280]{4,3,2,1,0:T(8,128)(2,1)}, bf16[1,1,8,32,1280]{4,3,2,1,0:T(8,128)(2,1)S(1)}, u32[]{:S(2)}, u32[]{:S(2)}) collective-permute-start(bf16[1,1,8,32,1280]{4,3,2,1,0:T(8,128)(2,1)} %param.9), channel_id=1, source_target_pairs={{0,2},{2,4},{4,6},{6,0},{1,3},{3,5},{5,7},{7,1},{8,10},{10,12},{12... | collective-permute-start | bytes 1966088 | tf_op jit(solution)/shard_map/ppermute | solution.py:103
  9.6 42.0 %collective-permute-start.8 = (bf16[9,1280,80]{1,2,0:T(8,128)(2,1)}, bf16[9,1280,80]{1,2,0:T(8,128)(2,1)}, u32[]{:S(2)}, u32[]{:S(2)}) collective-permute-start(bf16[9,1280,80]{1,2,0:T(8,128)(2,1)} %param.10), channel_id=1, source_target_pairs={{0,16},{8,24},{16,0},{24,8},{1,17},{9,25},{17,1},{25,9},{2,18},{10... | collective-permute-start | bytes 5529608 | tf_op jit(solution)/shard_map/ppermute | solution.py:22
  26.6 17.8 %copy-start.3 = (bf16[1,1,8,32,1280]{4,3,2,1,0:T(8,128)(2,1)}, bf16[1,1,8,32,1280]{4,3,2,1,0:T(8,128)(2,1)S(1)}, u32[]{:S(2)}) copy-start(bf16[1,1,8,32,1280]{4,3,2,1,0:T(8,128)(2,1)S(1)} %collective-permute-done) | copy-start | bytes 1966084
  26.6 17.8 %collective-permute-start.1 = (bf16[1,1,8,32,1280]{4,3,2,1,0:T(8,128)(2,1)S(1)}, bf16[1,1,8,32,1280]{4,3,2,1,0:T(8,128)(2,1)}, u32[]{:S(2)}, u32[]{:S(2)}) collective-permute-start(bf16[1,1,8,32,1280]{4,3,2,1,0:T(8,128)(2,1)S(1)} %collective-permute-done), channel_id=1, source_target_pairs={{0,2},{2,4},{4,6},{6,0},{1,3},{3,5},{5,7},{7,1},{8,10},{10,12},{12... | collective-permute-start | bytes 1966088 | tf_op jit(solution)/shard_map/ppermute | solution.py:103
  26.6 53.2 %collective-permute-start.7 = (bf16[9,1280,80]{1,2,0:T(8,128)(2,1)}, bf16[9,1280,80]{1,2,0:T(8,128)(2,1)}, u32[]{:S(2)}, u32[]{:S(2)}) collective-permute-start(bf16[9,1280,80]{1,2,0:T(8,128)(2,1)} %param.10), channel_id=1, source_target_pairs={{0,8},{8,0},{16,24},{24,16},{1,9},{9,1},{17,25},{25,17},{2,10},{10... | collective-permute-start | bytes 5529608 | tf_op jit(solution)/shard_map/ppermute | solution.py:23
  44.4 17.1 %collective-permute-start.2 = (bf16[1,1,8,32,1280]{4,3,2,1,0:T(8,128)(2,1)}, bf16[1,1,8,32,1280]{4,3,2,1,0:T(8,128)(2,1)S(1)}, u32[]{:S(2)}, u32[]{:S(2)}) collective-permute-start(bf16[1,1,8,32,1280]{4,3,2,1,0:T(8,128)(2,1)} %collective-permute-done.1), channel_id=1, source_target_pairs={{0,2},{2,4},{4,6},{6,0},{1,3},{3,5},{5,7},{7,1},{8,10},{10,12},{12... | collective-permute-start | bytes 1966088 | tf_op jit(solution)/shard_map/ppermute | solution.py:103
  51.6 28.3 %collective-permute-start.9 = (bf16[9,1280,80]{1,2,0:T(8,128)(2,1)}, bf16[9,1280,80]{1,2,0:T(8,128)(2,1)}, u32[]{:S(2)}, u32[]{:S(2)}) collective-permute-start(bf16[9,1280,80]{1,2,0:T(8,128)(2,1)} %collective-permute-done.8), channel_id=1, source_target_pairs={{0,8},{8,0},{16,24},{24,16},{1,9},{9,1},{17,25},{25,17},{2,10},{10... | collective-permute-start | bytes 5529608 | tf_op jit(solution)/shard_map/ppermute | solution.py:24
  61.5 8.9 %copy-start.6 = (f32[1280]{0:T(1024)S(1)}, f32[1280]{0:T(1024)}, u32[]{:S(2)}) copy-start(f32[1280]{0:T(1024)} %param.13) | copy-start | bytes 15364
  61.6 8.9 %copy-start.7 = (f32[1280]{0:T(1024)S(1)}, f32[1280]{0:T(1024)}, u32[]{:S(2)}) copy-start(f32[1280]{0:T(1024)} %param.12) | copy-start | bytes 15364
  62.6 6.2 %collective-permute-start.4 = (f32[1,32]{1,0:T(1,128)S(1)}, f32[1,32]{1,0:T(1,128)S(1)}, u32[]{:S(2)}, u32[]{:S(2)}) collective-permute-start(f32[1,32]{1,0:T(1,128)S(1)} %bitcast.227), channel_id=1, source_target_pairs={{0,1},{1,0},{2,3},{3,2},{4,5},{5,4},{6,7},{7,6},{8,9},{9,8},{10,11... | collective-permute-start | bytes 392 | tf_op jit(solution)/shard_map/ppermute | solution.py:13
  64.0 6.0 %collective-permute-start.5 = (f32[1,32]{1,0:T(1,128)S(1)}, f32[1,32]{1,0:T(1,128)S(1)}, u32[]{:S(2)}, u32[]{:S(2)}) collective-permute-start(f32[1,32]{1,0:T(1,128)S(1)} %bitcast.228), channel_id=1, source_target_pairs={{0,1},{1,0},{2,3},{3,2},{4,5},{5,4},{6,7},{7,6},{8,9},{9,8},{10,11... | collective-permute-start | bytes 392 | tf_op jit(solution)/shard_map/ppermute | solution.py:13
  64.9 7.7 %collective-permute-start.3 = (bf16[1,4,1,32,1280]{4,3,2,1,0:T(8,128)(2,1)S(1)}, bf16[1,4,1,32,1280]{4,3,2,1,0:T(8,128)(2,1)}, u32[]{:S(2)}, u32[]{:S(2)}) collective-permute-start(bf16[1,4,1,32,1280]{4,3,2,1,0:T(8,128)(2,1)S(1)} %get-tuple-element.31), channel_id=1, source_target_pairs={{0,1},{2,3},{4,5},{6,7},{8,9},{10,11},{12,13},{14,15},{16,17},{18,... | collective-permute-start | bytes 983048 | tf_op jit(solution)/shard_map/ppermute | solution.py:110
  68.8 9.1 %collective-permute-start.6 = (bf16[1,4,1,32,1280]{4,3,2,1,0:T(8,128)(2,1)S(1)}, bf16[1,4,1,32,1280]{4,3,2,1,0:T(8,128)(2,1)}, u32[]{:S(2)}, u32[]{:S(2)}) collective-permute-start(bf16[1,4,1,32,1280]{4,3,2,1,0:T(8,128)(2,1)S(1)} %get-tuple-element.32), channel_id=1, source_target_pairs={{1,0},{3,2},{5,4},{7,6},{9,8},{11,10},{13,12},{15,14},{17,16},{19,... | collective-permute-start | bytes 983048 | tf_op jit(solution)/shard_map/ppermute | solution.py:111
  105.2 3.6 %collective-permute-start.10 = (f32[8]{0:T(128)S(1)}, f32[8]{0:T(128)S(1)}, u32[]{:S(2)}, u32[]{:S(2)}) collective-permute-start(f32[8]{0:T(128)S(1)} %reduce_sum.78), channel_id=1, source_target_pairs={{0,1},{1,0},{2,3},{3,2},{4,5},{5,4},{6,7},{7,6},{8,9},{9,8},{10,11... | collective-permute-start | bytes 104 | tf_op jit(solution)/shard_map/ppermute | solution.py:13
  105.5 3.6 %collective-permute-start.11 = (f32[8]{0:T(128)S(1)}, f32[8]{0:T(128)S(1)}, u32[]{:S(2)}, u32[]{:S(2)}) collective-permute-start(f32[8]{0:T(128)S(1)} %reduce_sum.81), channel_id=1, source_target_pairs={{0,1},{1,0},{2,3},{3,2},{4,5},{5,4},{6,7},{7,6},{8,9},{9,8},{10,11... | collective-permute-start | bytes 104 | tf_op jit(solution)/shard_map/ppermute | solution.py:13
  110.9 10.3 %collective-permute-start.13 = (bf16[3,1280,80]{1,2,0:T(8,128)(2,1)S(1)}, bf16[3,1280,80]{1,2,0:T(8,128)(2,1)}, u32[]{:S(2)}, u32[]{:S(2)}) collective-permute-start(bf16[3,1280,80]{1,2,0:T(8,128)(2,1)S(1)} %copy-done.5), channel_id=1, source_target_pairs={{0,16},{8,24},{16,0},{24,8},{1,17},{9,25},{17,1},{25,9},{2,18},{10... | collective-permute-start | bytes 1843208 | tf_op jit(solution)/shard_map/ppermute | solution.py:22
  112.4 11.0 %collective-permute-start.12 = (bf16[3,1280,80]{1,2,0:T(8,128)(2,1)S(1)}, bf16[3,1280,80]{1,2,0:T(8,128)(2,1)}, u32[]{:S(2)}, u32[]{:S(2)}) collective-permute-start(bf16[3,1280,80]{1,2,0:T(8,128)(2,1)S(1)} %copy-done.5), channel_id=1, source_target_pairs={{0,8},{8,0},{16,24},{24,16},{1,9},{9,1},{17,25},{25,17},{2,10},{10... | collective-permute-start | bytes 1843208 | tf_op jit(solution)/shard_map/ppermute | solution.py:23
  121.2 3.8 %collective-permute-start.14 = (bf16[3,1280,80]{1,2,0:T(8,128)(2,1)}, bf16[3,1280,80]{1,2,0:T(8,128)(2,1)}, u32[]{:S(2)}, u32[]{:S(2)}) collective-permute-start(bf16[3,1280,80]{1,2,0:T(8,128)(2,1)} %collective-permute-done.13), channel_id=1, source_target_pairs={{0,8},{8,0},{16,24},{24,16},{1,9},{9,1},{17,25},{25,17},{2,10},{10... | collective-permute-start | bytes 1843208 | tf_op jit(solution)/shard_map/ppermute | solution.py:24
  183.8 16.4 %collective-permute-start.15 = (bf16[1,8,32,320]{3,2,1,0:T(8,128)(2,1)}, bf16[1,8,32,320]{3,2,1,0:T(8,128)(2,1)S(1)}, u32[]{:S(2)}, u32[]{:S(2)}) collective-permute-start(bf16[1,8,32,320]{3,2,1,0:T(8,128)(2,1)} %get-tuple-element.35), channel_id=1, source_target_pairs={{0,2},{2,4},{4,6},{6,0},{1,3},{3,5},{5,7},{7,1},{8,10},{10,12},{12... | collective-permute-start | bytes 491528 | tf_op jit(solution)/shard_map/ppermute | solution.py:217
  183.9 28.2 %collective-permute-start.16 = (bf16[1,8,32,320]{3,2,1,0:T(8,128)(2,1)}, bf16[1,8,32,320]{3,2,1,0:T(8,128)(2,1)S(1)}, u32[]{:S(2)}, u32[]{:S(2)}) collective-permute-start(bf16[1,8,32,320]{3,2,1,0:T(8,128)(2,1)} %get-tuple-element.34), channel_id=1, source_target_pairs={{0,4},{2,6},{4,0},{6,2},{1,5},{3,7},{5,1},{7,3},{8,12},{10,14},{12... | collective-permute-start | bytes 491528 | tf_op jit(solution)/shard_map/ppermute | solution.py:217
  185.2 38.7 %collective-permute-start.17 = (bf16[1,8,32,320]{3,2,1,0:T(8,128)(2,1)S(1)}, bf16[1,8,32,320]{3,2,1,0:T(8,128)(2,1)S(1)}, u32[]{:S(2)}, u32[]{:S(2)}) collective-permute-start(bf16[1,8,32,320]{3,2,1,0:T(8,128)(2,1)S(1)} %get-tuple-element.33), channel_id=1, source_target_pairs={{0,6},{2,0},{4,2},{6,4},{1,7},{3,1},{5,3},{7,5},{8,14},{10,8},{12,... | collective-permute-start | bytes 491528 | tf_op jit(solution)/shard_map/ppermute | solution.py:217
  224.2 13.7 %copy-start.8 = (f32[1280]{0:T(1024)S(1)}, f32[1280]{0:T(1024)}, u32[]{:S(2)}) copy-start(f32[1280]{0:T(1024)} %param.17) | copy-start | bytes 15364
  (4 other events, 11.9 us)
Sparse Core Ops, SparseCore 0:
  111.0 62.1 all-gather.2
